TPU v7x, 256 devices: a whole 4x4x8 slice. The times are simulated.
256 devices in a mesh: expert: 32 (over z_lo, x, core), replica: 8 (over z_hi, y).
Axes of the slice: x: 4, y: 4, z: 8 (z_hi: 2, z_lo: 4; z = z_hi * 4 + z_lo), core: 2. Of those that a mesh axis runs over, the one named last changes fastest.
Arguments:
- tokens: bfloat16 [2048, 4096], P(('expert', 'replica')), may hold values from -6 to 6
- expert_ids: int32 [2048, 8], P(('expert', 'replica')), may hold values from 0 to 31, as said below
- gate_weights: float32 [2048, 8], P(('expert', 'replica')), may hold values from 0.1 to 1
- expert_holder: int32 [32], replicated, may hold values from 0 to 31, each once
- swap_pairs: int32 [8, 2], replicated, may hold values from 0 to 31, as said below
- capacity: int32 [32], replicated, may hold values from 2 to 4, as said below
- w_gate: bfloat16 [32, 1536, 4096], P('expert', 'replica'), may hold values from -0.09375 to 0.09375
- w_up: bfloat16 [32, 1536, 4096], P('expert', 'replica'), may hold values from -0.09375 to 0.09375
- w_down: bfloat16 [32, 1536, 4096], P('expert', 'replica'), may hold values from -0.15625 to 0.15625
Outputs:
- moe_output: bfloat16 [2048, 4096], P(('expert', 'replica'))
- moved_gate: bfloat16 [32, 1536, 4096], P('expert', 'replica')
- moved_up: bfloat16 [32, 1536, 4096], P('expert', 'replica')
- moved_down: bfloat16 [32, 1536, 4096], P('expert', 'replica')
- expert_peak: float32 [32], P('expert')
Inputs may be any that keep to these rules, and one draw needn't show every extreme that they name: `expert_ids`: each token names 8 different experts; among one device's 8 tokens no expert is named more than 4 times, and one expert is named exactly 4 times by the tokens of every device. `swap_pairs`: no index appears twice; the two indices of every pair differ by 16. The expert named 4 times by every device has capacity 4. `expert_holder`: each index of the expert axis holds one expert.
All inputs are finite; a program needn't handle non-finite values.
Results may differ from a plain program's by a relative error of at most 0.014.
Values may be sent and summed in bfloat16 or wider, within the bound.
No kernel may reach another device: no remote copies, remote signals or barrier semaphores. Data moves between devices by JAX's collectives and lax.ppermute only.
A program may use at most 128 MiB of HBM per device.

v0:
```python
import jax
import jax.numpy as jnp
from jax import lax
from jax.sharding import PartitionSpec as P

TOPK = 8
CAP = 4


def pair_partner(swap_pairs, device_count):
    devices = jnp.arange(device_count, dtype=jnp.int32)
    first_dev = swap_pairs[:, 0:1]
    second_dev = swap_pairs[:, 1:2]
    offsets = jnp.where(devices[None, :] == first_dev, second_dev - first_dev, 0)
    offsets = offsets + jnp.where(devices[None, :] == second_dev, first_dev - second_dev, 0)
    return devices + jnp.sum(offsets, axis=0)


def table_lookup(values_table, positions):
    matches = positions[..., None] == jnp.arange(values_table.shape[0], dtype=jnp.int32)
    return jnp.sum(jnp.where(matches, values_table, 0), axis=-1)


def route_slots(expert_ids, holder_now, capacity):
    expert_count = holder_now.shape[0]
    flat_ids = expert_ids.reshape(-1)
    chosen = (flat_ids[:, None] == jnp.arange(expert_count, dtype=jnp.int32)[None, :]).astype(
        jnp.int32
    )
    earlier = jnp.cumsum(chosen, axis=0) - chosen
    ranking = jnp.sum(earlier * chosen, axis=1)
    slot_kept = ranking < table_lookup(capacity, flat_ids)
    target = table_lookup(holder_now, flat_ids)
    slot_ids = jnp.where(slot_kept, target * CAP + ranking, -1)
    matched = slot_ids[None, :] == jnp.arange(expert_count * CAP, dtype=jnp.int32)[:, None]
    owners = jnp.arange(flat_ids.shape[0], dtype=jnp.int32) // TOPK
    source = jnp.sum(jnp.where(matched, owners[None, :], 0), axis=1)
    filled = jnp.any(matched, axis=1)
    return (jnp.maximum(slot_ids, 0), slot_kept, source, filled)


def expert_hidden(row_block, gate_local, up_local):
    leading = row_block.shape[:-1]
    row_matrix = row_block.reshape(-1, row_block.shape[-1])
    contract = (((1,), (1,)), ((), ()))
    gate_value = lax.dot_general(
        row_matrix, gate_local, contract, preferred_element_type=jnp.float32
    )
    up_value = lax.dot_general(row_matrix, up_local, contract, preferred_element_type=jnp.float32)
    hidden = (jax.nn.silu(gate_value) * up_value).astype(jnp.bfloat16)
    return hidden.reshape(leading + (gate_local.shape[0],))


def shards(
    tokens, expert_ids, gate_weights, expert_holder, swap_pairs, capacity, w_gate, w_up, w_down
):
    experts = lax.axis_size("expert")
    replicas = lax.axis_size("replica")
    tok_rows, width = tokens.shape
    partner = pair_partner(swap_pairs, experts)
    me = lax.axis_index("expert")
    swapped = lax.dynamic_index_in_dim(partner, me, 0, keepdims=False) != me
    half = experts // 2
    ring = [(d, (d + half) % experts) for d in range(experts)]
    arrived = tuple((lax.ppermute(w, "expert", ring) for w in (w_gate, w_up, w_down)))
    moved_gate, moved_up, moved_down = (
        jnp.where(swapped, got, own) for got, own in zip(arrived, (w_gate, w_up, w_down))
    )
    gate_local, up_local, down_local = (w_gate[0], w_up[0], w_down[0])
    group_tokens, group_ids = (
        lax.all_gather(tokens, "replica", axis=0, tiled=True),
        lax.all_gather(expert_ids, "replica", axis=0, tiled=True),
    )
    group_ids = group_ids.reshape(replicas, tok_rows, TOPK)
    slot_all, kept_all, source_all, filled_all = jax.vmap(route_slots, in_axes=(0, None, None))(
        group_ids, expert_holder, capacity
    )
    starts = jnp.arange(replicas, dtype=jnp.int32)[:, None] * tok_rows
    picked = jnp.take(group_tokens, source_all + starts, axis=0)
    outgoing = jnp.where(filled_all[:, :, None], picked, jnp.zeros((), jnp.bfloat16))
    hidden = expert_hidden(
        lax.all_to_all(
            outgoing.reshape(replicas, experts, CAP, width),
            "expert",
            split_axis=1,
            concat_axis=1,
            tiled=True,
        ),
        gate_local,
        up_local,
    )
    replica_index = lax.axis_index("replica")
    slot_of = lax.dynamic_index_in_dim(slot_all, replica_index, 0, keepdims=False)
    slot_kept = lax.dynamic_index_in_dim(kept_all, replica_index, 0, keepdims=False)
    hidden_rows = hidden.reshape(-1, hidden.shape[-1])
    local_peak = jnp.max(jnp.abs(hidden_rows)).astype(jnp.float32)
    summed = lax.psum_scatter(
        jnp.dot(hidden_rows, down_local, preferred_element_type=jnp.float32).astype(jnp.bfloat16),
        "replica",
        scatter_dimension=0,
        tiled=True,
    )
    results = summed.reshape(experts, CAP, width)
    returned = lax.all_to_all(results, "expert", split_axis=0, concat_axis=0, tiled=True)
    fetched = jnp.take(returned.reshape(experts * CAP, width), slot_of, axis=0).reshape(
        tok_rows, TOPK, width
    )
    scales = jnp.where(slot_kept, gate_weights.reshape(-1), jnp.float32(0.0)).reshape(
        tok_rows, TOPK, 1
    )
    moe_output = jnp.sum(scales * fetched, axis=1).astype(jnp.bfloat16)
    group_peak = lax.pmax(local_peak, "replica")
    expert_peak = jnp.where(swapped, lax.ppermute(group_peak, "expert", ring), group_peak)
    return (moe_output, moved_gate, moved_up, moved_down, expert_peak.reshape(1))


def solution(mesh):
    placed = (
        P(("expert", "replica"), None),
        P(("expert", "replica"), None),
        P(("expert", "replica"), None),
        P(),
        P(),
        P(),
        P("expert", "replica", None),
        P("expert", "replica", None),
        P("expert", "replica", None),
    )
    return jax.shard_map(
        shards,
        mesh=mesh,
        in_specs=placed,
        out_specs=(
            P(("expert", "replica"), None),
            P("expert", "replica", None),
            P("expert", "replica", None),
            P("expert", "replica", None),
            P("expert"),
        ),
        check_vma=False,
    )
```

profile of v0, /device:TPU:4, one launch (start us, length us, event | category | flops | bytes accessed | tf_op | source)
XLA Modules:
  0.0 756.1 jit_solution(8081594906752745250)
XLA Ops:
  7.2 46.4 %all_gather.6 = s32[64,8]{1,0:T(8,128)S(1)} all-gather(s32[8,8]{1,0:T(8,128)} %param.10), channel_id=1, replica_groups=mesh['expert'=32,'replica'=8] {'replica'}, dimensions={0}, use_global_device_ids=true | all-gather | bytes 2304 | tf_op jit(solution)/shard_map/all_gather | solution.py:72
  53.8 1.4 fusion.20
  55.1 3.0 select_reduce_fusion.1
  58.2 0.2 fusion.13
  58.4 0.2 select_reduce_fusion
  58.7 44.8 %all_gather.7 = bf16[64,4096]{1,0:T(8,128)(2,1)S(1)} all-gather(bf16[8,4096]{1,0:T(8,128)(2,1)} %param.9), channel_id=1, replica_groups=mesh['expert'=32,'replica'=8] {'replica'}, dimensions={0}, use_global_device_ids=true | all-gather | bytes 589824 | tf_op jit(solution)/shard_map/all_gather | solution.py:71
  103.5 7.7 %gather_fusion = bf16[1024,4096]{1,0:T(8,128)(2,1)} fusion(bf16[64,4096]{1,0:T(8,128)(2,1)S(1)} %all_gather.7, s32[1024]{0:T(1024)S(1)} %fusion.18), kind=kCustom, calls=%fused_computation | custom fusion | bytes 16781312 | tf_op jit(solution)/shard_map/jit(_take)/gather | solution.py:79
  111.3 13.1 %gather.13 = bf16[8,32,4,4096]{3,2,1,0:T(4,128)(2,1)} reshape(bf16[1024,4096]{1,0:T(8,128)(2,1)} %gather_fusion) | data formatting | bytes 16777216 | tf_op jit(solution)/shard_map/jit(_take)/gather | solution.py:79
  124.5 0.2 copy.49
  124.8 0.3 copy.46
  125.1 7.3 fusion
  132.4 189.9 %all_to_all.10 = bf16[8,32,4,4096]{3,2,0,1:T(4,128)(2,1)S(1)} all-to-all(bf16[8,32,4,4096]{3,2,0,1:T(4,128)(2,1)S(1)} %fusion), channel_id=1, replica_groups=mesh['expert'=32,'replica'=8] {'expert'}, dimensions={1} | all-to-all | bytes 16777216 | tf_op jit(solution)/shard_map/all_to_all | solution.py:82
  322.3 6.1 copy.51
  328.4 12.5 %reshape.149 = bf16[1024,4096]{1,0:T(8,128)(2,1)} reshape(bf16[8,32,4,4096]{3,2,1,0:T(4,128)(2,1)} %copy.51) | data formatting | bytes 16777216 | tf_op jit(solution)/shard_map/reshape | solution.py:44
  340.9 6.8 fusion.4
  347.8 5.1 abs_reduce_fusion
  352.9 5.6 convolution_convert_fusion
  358.7 2.9 collective-permute-start.1
  361.8 0.6 dynamic_slice.14
  363.1 0.2 fusion.16
  363.3 0.2 dynamic-slice_reduce_fusion
  363.7 233.9 %collective-permute-done.2 = bf16[1,192,4096]{2,1,0:T(8,128)(2,1)S(1)} collective-permute-done((bf16[1,192,4096]{2,1,0:T(8,128)(2,1)S(1)}, bf16[1,192,4096]{2,1,0:T(8,128)(2,1)S(1)}, u32[]{:S(2)}, u32[]{:S(2)}) %collective-permute-start.2) | collective-permute-done | bytes 1572896 | tf_op jit(solution)/shard_map/ppermute | solution.py:65
  597.6 1.3 broadcast_select_fusion
  598.9 2.3 reshape.150
  601.1 99.3 %all-to-all-start.1 = ((bf16[32,4,4096]{2,1,0:T(4,128)(2,1)}), bf16[32,4,4096]{2,1,0:T(4,128)(2,1)S(1)}, u32[]{:S(2)}, u32[]{:S(2)}) async-start(bf16[32,4,4096]{2,1,0:T(4,128)(2,1)} %reshape.150), calls=%async_computation.2 | async-start | bytes 2097152 | tf_op jit(solution)/shard_map/all_to_all | solution.py:104
  700.5 2.7 broadcast_select_fusion.1
  703.2 2.7 broadcast_select_fusion.2
  705.9 34.1 %pmax.7 = f32[]{:T(128)} all-reduce(bf16[]{:T(256)} %get-tuple-element.13), channel_id=1, replica_groups=mesh['expert'=32,'replica'=8] {'replica'}, use_global_device_ids=true, to_apply=%region_10.11 | all-reduce | flops 1 | bytes 6 | tf_op jit(solution)/shard_map/pmax | solution.py:112
  740.0 4.6 collective-permute-done.3
  745.9 0.3 reshape.151
  746.2 0.9 gather_fusion.1
  747.1 1.1 multiply_reduce_fusion
  (37 shorter events, 1.3 us)
Async XLA Ops:
  7.2 591.7 %reduce-scatter.2.cloned.1.call-start = ((), (), s32[]{:S(2)}) async-start(), calls=%async_computation.3 | async-start | bytes 9437184 | tf_op jit(solution)/shard_map/reduce_scatter | solution.py:97
  340.9 6.9 copy-start
  347.8 5.1 copy-start.1
  358.6 3.1 copy-start.3
  358.6 5.1 copy-start.2
  358.6 239.0 %collective-permute-start.2 = (bf16[1,192,4096]{2,1,0:T(8,128)(2,1)S(1)}, bf16[1,192,4096]{2,1,0:T(8,128)(2,1)S(1)}, u32[]{:S(2)}, u32[]{:S(2)}) collective-permute-start(bf16[1,192,4096]{2,1,0:T(8,128)(2,1)S(1)} %copy-done.1), channel_id=1, source_target_pairs={{0,128},{8,136},{16,144},{24,152},{32,160},{40,168},{48,176},{56,1... | collective-permute-start | bytes 4718600 | tf_op jit(solution)/shard_map/ppermute | solution.py:65
  358.7 341.8 %collective-permute-start.1 = (bf16[1,192,4096]{2,1,0:T(8,128)(2,1)}, bf16[1,192,4096]{2,1,0:T(8,128)(2,1)}, u32[]{:S(2)}, u32[]{:S(2)}) collective-permute-start(bf16[1,192,4096]{2,1,0:T(8,128)(2,1)} %param.16), channel_id=1, source_target_pairs={{0,128},{8,136},{16,144},{24,152},{32,160},{40,168},{48,176},{56,1... | collective-permute-start | bytes 4718600 | tf_op jit(solution)/shard_map/ppermute | solution.py:65
  361.6 341.6 %collective-permute-start = (bf16[1,192,4096]{2,1,0:T(8,128)(2,1)}, bf16[1,192,4096]{2,1,0:T(8,128)(2,1)}, u32[]{:S(2)}, u32[]{:S(2)}) collective-permute-start(bf16[1,192,4096]{2,1,0:T(8,128)(2,1)} %param.15), channel_id=1, source_target_pairs={{0,128},{8,136},{16,144},{24,152},{32,160},{40,168},{48,176},{56,1... | collective-permute-start | bytes 4718600 | tf_op jit(solution)/shard_map/ppermute | solution.py:65
  601.1 144.8 %all-to-all-start.1 = ((bf16[32,4,4096]{2,1,0:T(4,128)(2,1)}), bf16[32,4,4096]{2,1,0:T(4,128)(2,1)S(1)}, u32[]{:S(2)}, u32[]{:S(2)}) async-start(bf16[32,4,4096]{2,1,0:T(4,128)(2,1)} %reshape.150), calls=%async_computation.2 | async-start | bytes 2097152 | tf_op jit(solution)/shard_map/all_to_all | solution.py:104
  740.0 4.6 collective-permute-start.3
Sparse Core Ops, SparseCore 0:
  358.7 222.3 reduce-scatter.1
where the time goes:
time: 757 us; the launch traced here: 756 us
  blocking collectives  315 us (42%)
  waiting for transfers between devices  238 us (31%)
  starting transfers between devices  102 us (13%)
  local copies, waits for them, and re-layouts  44.8 us (6%)
  other arithmetic  20.3 us (3%)
  matrix products  17.6 us (2%)
  between operations  17.3 us (2%)
    ppermute x3, waiting for transfers between devices, shards(): lax.ppermute(w, 'expert', ring)  234 us
    all_to_all x1, blocking collectives, shards(): lax.all_to_all(outgoing.reshape(replicas, experts, CAP, width), 'expert',...  190 us
    all_to_all x1, starting transfers between devices, shards(): lax.all_to_all(results, 'expert', split_axis=0, concat_axis=0, tiled=True)  99.3 us
    all_gather x1, blocking collectives, shards(): lax.all_gather(expert_ids, 'replica', axis=0, tiled=True)  46.4 us
    all_gather x1, blocking collectives, shards(): lax.all_gather(tokens, 'replica', axis=0, tiled=True)  44.8 us
    pmax x1, blocking collectives, shards(): group_peak = lax.pmax(local_peak, 'replica')  34.1 us
    gather x2, local copies, waits for them, and re-layouts, shards(): picked = jnp.take(group_tokens, source_all + starts, axis=0)  20.8 us
  transfers between devices with their start and end apart: 6, of which 2 were waited for; matrix products, arithmetic and copies ran while one was open for 1% of the time, Pallas kernels for 0%

commit v1 on v0

--- a/solution.py
+++ b/solution.py
@@ -67,9 +67,18 @@
         jnp.where(swapped, got, own) for got, own in zip(arrived, (w_gate, w_up, w_down))
     )
     gate_local, up_local, down_local = (w_gate[0], w_up[0], w_down[0])
+    set_record = lambda u_in, which_dim: jnp.concatenate(
+        jax.lax.all_to_all(
+            jnp.stack([u_in] * jax.lax.axis_size("replica"), axis=0),
+            axis_name="replica",
+            split_axis=0,
+            concat_axis=0,
+        ),
+        which_dim,
+    )
     group_tokens, group_ids = (
         lax.all_gather(tokens, "replica", axis=0, tiled=True),
-        lax.all_gather(expert_ids, "replica", axis=0, tiled=True),
+        set_record(expert_ids, 0),
     )
     group_ids = group_ids.reshape(replicas, tok_rows, TOPK)
     slot_all, kept_all, source_all, filled_all = jax.vmap(route_slots, in_axes=(0, None, None))(

time: 757 us -> 723 us (0.955)
  blocking collectives: 315 us -> 269 us
  starting transfers between devices: 102 us -> 113 us
    all_gather x1 -> x0, blocking collectives: 46.4 us -> none  [shards(): lax.all_gather(expert_ids, 'replica', axis=0, tiled=True)]
    all_to_all x0 -> x1, starting transfers between devices: none -> 11.1 us  [shards(): jax.lax.all_to_all(jnp.stack([u_in] * jax.lax.axis_size('replica'), axis=...]
  transfers between devices with their start and end apart: 6 -> 7, of which waited for: 2 -> 2; matrix products, arithmetic and copies ran while one was open for 1% -> 1% of each run, Pallas kernels for 0% -> 0%
where the time goes in v1:
time: 723 us; the launch traced here: 722 us
  blocking collectives  269 us (37%)
  waiting for transfers between devices  238 us (33%)
  starting transfers between devices  113 us (16%)
  local copies, waits for them, and re-layouts  46 us (6%)
  other arithmetic  20.3 us (3%)
  matrix products  17.6 us (2%)
  between operations  17.3 us (2%)
    ppermute x3, waiting for transfers between devices, shards(): lax.ppermute(w, 'expert', ring)  234 us
    all_to_all x1, blocking collectives, shards(): lax.all_to_all(outgoing.reshape(replicas, experts, CAP, width), 'expert',...  189 us
    all_to_all x1, starting transfers between devices, shards(): lax.all_to_all(results, 'expert', split_axis=0, concat_axis=0, tiled=True)  99.2 us
    all_gather x1, blocking collectives, shards(): lax.all_gather(tokens, 'replica', axis=0, tiled=True)  45.8 us
    pmax x1, blocking collectives, shards(): group_peak = lax.pmax(local_peak, 'replica')  34.1 us
    gather x2, local copies, waits for them, and re-layouts, shards(): picked = jnp.take(group_tokens, source_all + starts, axis=0)  20.8 us
  transfers between devices with their start and end apart: 7, of which 2 were waited for; matrix products, arithmetic and copies ran while one was open for 1% of the time, Pallas kernels for 0%

profile of v1, /device:TPU:4, one launch (start us, length us, event | category | flops | bytes accessed | tf_op | source)
XLA Modules:
  0.0 722.4 jit_solution(6869533828864325848)
XLA Ops:
  7.2 1.3 stack.2
  8.5 11.1 %all-to-all-start = ((s32[8,8,8]{2,1,0:T(8,128)}), s32[8,8,8]{2,1,0:T(8,128)S(1)}, u32[]{:S(2)}, u32[]{:S(2)}) async-start(s32[8,8,8]{2,1,0:T(8,128)} %stack.2), calls=%async_computation | async-start | bytes 65536 | tf_op jit(solution)/shard_map/all_to_all | solution.py:71
  19.6 45.8 %all_gather.3 = bf16[64,4096]{1,0:T(8,128)(2,1)S(1)} all-gather(bf16[8,4096]{1,0:T(8,128)(2,1)} %param.9), channel_id=1, replica_groups=mesh['expert'=32,'replica'=8] {'replica'}, dimensions={0}, use_global_device_ids=true | all-gather | bytes 589824 | tf_op jit(solution)/shard_map/all_gather | solution.py:80
  65.5 1.4 fusion.20
  66.9 3.0 select_reduce_fusion.1
  70.0 0.2 fusion.13
  70.5 7.7 %gather_fusion = bf16[1024,4096]{1,0:T(8,128)(2,1)} fusion(bf16[64,4096]{1,0:T(8,128)(2,1)S(1)} %all_gather.3, s32[1024]{0:T(1024)S(1)} %fusion.18), kind=kCustom, calls=%fused_computation | custom fusion | bytes 16781312 | tf_op jit(solution)/shard_map/jit(_take)/gather | solution.py:88
  78.2 13.1 %gather.13 = bf16[8,32,4,4096]{3,2,1,0:T(4,128)(2,1)} reshape(bf16[1024,4096]{1,0:T(8,128)(2,1)} %gather_fusion) | data formatting | bytes 16777216 | tf_op jit(solution)/shard_map/jit(_take)/gather | solution.py:88
  91.5 0.2 copy.46
  91.8 0.3 copy.43
  92.1 7.3 %fusion = bf16[8,32,4,4096]{3,2,0,1:T(4,128)(2,1)S(1)} fusion(bf16[8,32,4,4096]{3,2,1,0:T(4,128)(2,1)} %gather.13, pred[8,32,4]{2,0,1:T(8,128)(4,1)S(1)} %copy.46, pred[8,32,4]{2,0,1:T(8,128)(4,1)S(1)} %copy.43), kind=kLoop, calls=%fused_computation.3 | loop fusion | flops 8388608 | bytes 16779264 | tf_op jit(solution)/shard_map/jit(_where)/select_n | solution.py:89
  99.4 189.3 %all_to_all.15 = bf16[8,32,4,4096]{3,2,0,1:T(4,128)(2,1)S(1)} all-to-all(bf16[8,32,4,4096]{3,2,0,1:T(4,128)(2,1)S(1)} %fusion), channel_id=1, replica_groups=mesh['expert'=32,'replica'=8] {'expert'}, dimensions={1} | all-to-all | bytes 16777216 | tf_op jit(solution)/shard_map/all_to_all | solution.py:91
  288.7 6.1 copy.48
  294.8 12.5 %reshape.151 = bf16[1024,4096]{1,0:T(8,128)(2,1)} reshape(bf16[8,32,4,4096]{3,2,1,0:T(4,128)(2,1)} %copy.48) | data formatting | bytes 16777216 | tf_op jit(solution)/shard_map/reshape | solution.py:44
  307.4 6.8 fusion.4
  314.2 5.1 abs_reduce_fusion
  319.4 5.6 convolution_convert_fusion
  325.1 2.9 collective-permute-start.1
  328.2 0.6 dynamic_slice.14
  329.5 0.2 fusion.16
  329.7 0.2 dynamic-slice_reduce_fusion
  330.1 233.9 %collective-permute-done.2 = bf16[1,192,4096]{2,1,0:T(8,128)(2,1)S(1)} collective-permute-done((bf16[1,192,4096]{2,1,0:T(8,128)(2,1)S(1)}, bf16[1,192,4096]{2,1,0:T(8,128)(2,1)S(1)}, u32[]{:S(2)}, u32[]{:S(2)}) %collective-permute-start.2) | collective-permute-done | bytes 1572896 | tf_op jit(solution)/shard_map/ppermute | solution.py:65
  564.0 1.3 broadcast_select_fusion
  565.3 2.3 reshape.152
  567.5 99.2 %all-to-all-start.2 = ((bf16[32,4,4096]{2,1,0:T(4,128)(2,1)}), bf16[32,4,4096]{2,1,0:T(4,128)(2,1)S(1)}, u32[]{:S(2)}, u32[]{:S(2)}) async-start(bf16[32,4,4096]{2,1,0:T(4,128)(2,1)} %reshape.152), calls=%async_computation.3 | async-start | bytes 2097152 | tf_op jit(solution)/shard_map/all_to_all | solution.py:113
  666.8 2.7 broadcast_select_fusion.1
  669.5 2.7 broadcast_select_fusion.2
  672.2 34.1 %pmax.7 = f32[]{:T(128)} all-reduce(bf16[]{:T(256)} %get-tuple-element.13), channel_id=1, replica_groups=mesh['expert'=32,'replica'=8] {'replica'}, use_global_device_ids=true, to_apply=%region_10.11 | all-reduce | flops 1 | bytes 6 | tf_op jit(solution)/shard_map/pmax | solution.py:121
  706.3 4.6 collective-permute-done.3
  712.2 0.3 reshape.153
  712.5 0.9 gather_fusion.1
  713.4 1.1 multiply_reduce_fusion
  (38 shorter events, 1.3 us)
Async XLA Ops:
  8.5 57.0 %all-to-all-start = ((s32[8,8,8]{2,1,0:T(8,128)}), s32[8,8,8]{2,1,0:T(8,128)S(1)}, u32[]{:S(2)}, u32[]{:S(2)}) async-start(s32[8,8,8]{2,1,0:T(8,128)} %stack.2), calls=%async_computation | async-start | bytes 65536 | tf_op jit(solution)/shard_map/all_to_all | solution.py:71
  19.6 545.7 %reduce-scatter.2.cloned.1.call-start = ((), (), s32[]{:S(2)}) async-start(), calls=%async_computation.4 | async-start | bytes 9437184 | tf_op jit(solution)/shard_map/reduce_scatter | solution.py:106
  307.4 6.9 copy-start
  314.2 5.1 copy-start.1
  325.0 3.1 copy-start.3
  325.0 5.1 copy-start.2
  325.0 239.0 %collective-permute-start.2 = (bf16[1,192,4096]{2,1,0:T(8,128)(2,1)S(1)}, bf16[1,192,4096]{2,1,0:T(8,128)(2,1)S(1)}, u32[]{:S(2)}, u32[]{:S(2)}) collective-permute-start(bf16[1,192,4096]{2,1,0:T(8,128)(2,1)S(1)} %copy-done.1), channel_id=1, source_target_pairs={{0,128},{8,136},{16,144},{24,152},{32,160},{40,168},{48,176},{56,1... | collective-permute-start | bytes 4718600 | tf_op jit(solution)/shard_map/ppermute | solution.py:65
  325.1 341.6 %collective-permute-start.1 = (bf16[1,192,4096]{2,1,0:T(8,128)(2,1)}, bf16[1,192,4096]{2,1,0:T(8,128)(2,1)}, u32[]{:S(2)}, u32[]{:S(2)}) collective-permute-start(bf16[1,192,4096]{2,1,0:T(8,128)(2,1)} %param.16), channel_id=1, source_target_pairs={{0,128},{8,136},{16,144},{24,152},{32,160},{40,168},{48,176},{56,1... | collective-permute-start | bytes 4718600 | tf_op jit(solution)/shard_map/ppermute | solution.py:65
  328.0 341.5 %collective-permute-start = (bf16[1,192,4096]{2,1,0:T(8,128)(2,1)}, bf16[1,192,4096]{2,1,0:T(8,128)(2,1)}, u32[]{:S(2)}, u32[]{:S(2)}) collective-permute-start(bf16[1,192,4096]{2,1,0:T(8,128)(2,1)} %param.15), channel_id=1, source_target_pairs={{0,128},{8,136},{16,144},{24,152},{32,160},{40,168},{48,176},{56,1... | collective-permute-start | bytes 4718600 | tf_op jit(solution)/shard_map/ppermute | solution.py:65
  567.5 144.6 %all-to-all-start.2 = ((bf16[32,4,4096]{2,1,0:T(4,128)(2,1)}), bf16[32,4,4096]{2,1,0:T(4,128)(2,1)S(1)}, u32[]{:S(2)}, u32[]{:S(2)}) async-start(bf16[32,4,4096]{2,1,0:T(4,128)(2,1)} %reshape.152), calls=%async_computation.3 | async-start | bytes 2097152 | tf_op jit(solution)/shard_map/all_to_all | solution.py:113
  706.3 4.6 collective-permute-start.3
Sparse Core Ops, SparseCore 0:
  325.1 222.2 reduce-scatter.1
